TPU v7x, 512 devices: a whole 4x8x8 slice. The times are simulated.
512 devices in a mesh: wide: 64 (over z, x, core), narrow: 8 (over y).
Axes of the slice: x: 4, y: 8, z: 8, core: 2. Of those that a mesh axis runs over, the one named last changes fastest.
Arguments:
- hidden_in: bfloat16 [16384, 2048], P('wide', 'narrow'), may hold values from -6 to 6
- segment_ids: int32 [16384], P('wide'), may hold values from 0 to 31, never falling along the last dimension, each value on 1 to 2048 neighbouring positions
- page_table: int32 [1024], P('wide'), may hold values from 0 to 1023, as said below
- wq: bfloat16 [2048, 2048], P('wide', 'narrow')
- wk: bfloat16 [2048, 2048], P('wide', 'narrow')
- wv: bfloat16 [2048, 2048], P('wide', 'narrow'), may hold values from -0.125 to 0.125
- wo: bfloat16 [2048, 2048], P('narrow', 'wide'), may hold values from -0.125 to 0.125
- wg: bfloat16 [2048, 4096], P('wide', 'narrow'), may hold values from -0.125 to 0.125
- wu: bfloat16 [2048, 4096], P('wide', 'narrow'), may hold values from -0.125 to 0.125
- wd: bfloat16 [4096, 2048], P('narrow', 'wide'), may hold values from -0.09375 to 0.09375
Outputs:
- result: bfloat16 [16384, 2048], P('wide', 'narrow')
- kv_cache: bfloat16 [2, 1024, 16, 2048], P(None, 'wide', None, 'narrow')
Inputs may be any that keep to these rules, and one draw needn't show every extreme that they name: `page_table`: entries 16 * w to 16 * (w + 1) - 1 of the table are a permutation of those same numbers, for every w.
All inputs are finite; a program needn't handle non-finite values.
Results may differ from a plain program's by a relative error of at most 0.017.
Values may be sent and summed in bfloat16 or wider, within the bound.
No kernel may reach another device: no remote copies, remote signals or barrier semaphores. Data moves between devices by JAX's collectives and lax.ppermute only.
A program may use at most 64 MiB of HBM per device.

v0:
```python
import jax
import jax.numpy as jnp
from jax import lax
from jax.sharding import PartitionSpec as P

HEAD_DIM = 128
REACH = 8
PAGE = 16
epsilon = 1e-05
rope_base = 10000.0


def shifted(value, axis, steps):
    count = lax.axis_size(axis)
    first, last = (max(0, -steps), min(count, count - steps))
    return lax.ppermute(value, axis, [(source, source + steps) for source in range(first, last)])


def norm_rows(source):
    widened = source.astype(jnp.float32)
    center = widened - jnp.mean(widened, axis=-1, keepdims=True)
    spread = jnp.mean(center * center, axis=-1, keepdims=True)
    return (center * lax.rsqrt(spread + epsilon)).astype(jnp.bfloat16)


def rotate(projected, positions):
    head_size = projected.shape[-1]
    half_dim = head_size // 2
    frequency = jnp.power(rope_base, -jnp.arange(half_dim, dtype=jnp.float32) * 2.0 / head_size)
    angles = positions.astype(jnp.float32)[:, None] * frequency[None, :]
    cosine = jnp.cos(angles)[:, None, :]
    sine_part = jnp.sin(angles)[:, None, :]
    first_half = projected[..., :half_dim]
    second_half = projected[..., half_dim:]
    return jnp.concatenate(
        [
            first_half * cosine - second_half * sine_part,
            second_half * cosine + first_half * sine_part,
        ],
        axis=-1,
    )


def add_rows(source, piece):
    return jnp.dot(source, piece, preferred_element_type=jnp.float32)


def per_device(hidden_in, segment_ids, page_table, wq, wk, wv, wo, wg, wu, wd):
    tok_rows = hidden_in.shape[0]
    wide_rank = lax.axis_index("wide")
    local_index = jnp.arange(tok_rows, dtype=jnp.int32)
    attn_width = wq.shape[1]
    ff_width = wg.shape[1]
    pieces = [wq, wk, wv, wo.T, wg, wu, wd.T]
    widths = [piece.shape[1] for piece in pieces]
    gathered = lax.all_gather(jnp.concatenate(pieces, axis=1), "wide", axis=0, tiled=True)
    offsets = [sum(widths[:k]) for k in range(len(widths))]
    full = [gathered[:, o : o + w] for o, w in zip(offsets, widths)]
    wq_all, wk_all, wv_all, wo_t, wg_all, wu_all, wd_t = full
    id_blocks = []
    for step_back in range(REACH, 0, -1):
        got = shifted(segment_ids, "wide", step_back)
        id_blocks.append(jnp.where(wide_rank >= step_back, got, -1))
    id_blocks.append(segment_ids)
    window_ids = jnp.concatenate(id_blocks, axis=0)
    window_len = window_ids.shape[0]
    lead = REACH * tok_rows
    window_index = jnp.arange(window_len, dtype=jnp.int32)
    same = window_ids[None, :] == segment_ids[:, None]
    allowed = same & (window_index[None, :] <= lead + local_index[:, None])
    earlier = same & (window_index[None, :] < lead + local_index[:, None])
    positions = jnp.sum(earlier.astype(jnp.int32), axis=1)
    whole = lax.all_gather(hidden_in, "narrow", axis=1, tiled=True)
    normed = norm_rows(whole)
    local_width = attn_width
    head_count = local_width // HEAD_DIM
    q_proj = add_rows(normed, wq_all)
    k_proj = add_rows(normed, wk_all)
    v_proj = add_rows(normed, wv_all)
    queries = rotate(q_proj.reshape(tok_rows, head_count, HEAD_DIM), positions).astype(jnp.bfloat16)
    keys_rot = rotate(k_proj.reshape(tok_rows, head_count, HEAD_DIM), positions).astype(
        jnp.bfloat16
    )
    values = v_proj.astype(jnp.bfloat16).reshape(tok_rows, head_count, HEAD_DIM)
    blocks = []
    for step_back in range(REACH, 0, -1):
        blocks.append(shifted((keys_rot, values), "wide", step_back))
    blocks.append((keys_rot, values))
    score_scale = HEAD_DIM ** (-0.5)
    key_all = jnp.concatenate([member[0] for member in blocks], axis=0)
    value_all = jnp.concatenate([member[1] for member in blocks], axis=0)
    scores = (
        jnp.einsum("qhd,khd->hqk", queries, key_all, preferred_element_type=jnp.float32)
        * score_scale
    )
    scores = jnp.where(allowed[None], scores, -1e30)
    row_peak = jnp.max(scores, axis=-1, keepdims=True)
    exps = jnp.where(allowed[None], jnp.exp(scores - row_peak), 0.0)
    attn_probs = (exps / jnp.sum(exps, axis=-1, keepdims=True)).astype(jnp.bfloat16)
    mixed = jnp.einsum("hqk,khd->qhd", attn_probs, value_all, preferred_element_type=jnp.float32)
    attended = mixed.astype(jnp.bfloat16).reshape(tok_rows, local_width)
    attn_terms = lax.dot_general(
        attended, wo_t, (((1,), (1,)), ((), ())), preferred_element_type=jnp.float32
    )
    attn_sum = lax.psum_scatter(
        attn_terms.astype(jnp.bfloat16), "narrow", scatter_dimension=1, tiled=True
    ).astype(jnp.float32)
    first_res = (hidden_in.astype(jnp.float32) + attn_sum).astype(jnp.bfloat16)
    whole_two = lax.all_gather(first_res, "narrow", axis=1, tiled=True)
    normed_two = norm_rows(whole_two)
    gate_proj = add_rows(normed_two, wg_all)
    up_proj = add_rows(normed_two, wu_all)
    hidden = (jax.nn.silu(gate_proj) * up_proj).astype(jnp.bfloat16)
    down_terms = lax.dot_general(
        hidden, wd_t, (((1,), (1,)), ((), ())), preferred_element_type=jnp.float32
    )
    down_sum = lax.psum_scatter(
        down_terms.astype(jnp.bfloat16), "narrow", scatter_dimension=1, tiled=True
    ).astype(jnp.float32)
    result = (first_res.astype(jnp.float32) + down_sum).astype(jnp.bfloat16)
    page_count = tok_rows // PAGE
    slots = page_table - wide_rank * page_count
    pairs = jnp.stack(
        [
            keys_rot.reshape(page_count, PAGE, local_width),
            values.reshape(page_count, PAGE, local_width),
        ],
        axis=0,
    )
    kv_cache = jnp.zeros_like(pairs).at[:, slots].set(pairs)
    return (result, kv_cache)


def solution(mesh):
    return jax.shard_map(
        per_device,
        mesh=mesh,
        in_specs=(
            P("wide", "narrow"),
            P("wide"),
            P("wide"),
            P("wide", "narrow"),
            P("wide", "narrow"),
            P("wide", "narrow"),
            P("narrow", "wide"),
            P("wide", "narrow"),
            P("wide", "narrow"),
            P("narrow", "wide"),
        ),
        out_specs=(P("wide", "narrow"), P(None, "wide", None, "narrow")),
        check_vma=False,
    )
```

profile of v0, /device:TPU:6, one launch (start us, length us, event | category | flops | bytes accessed | tf_op | source)
XLA Modules:
  0.0 365.4 jit_solution(13922790470429218336)
XLA Ops:
  13.8 4.3 %collective-permute-start.8 = (s32[256]{0:T(256)}, s32[256]{0:T(256)S(1)}, u32[]{:S(2)}, u32[]{:S(2)}) collective-permute-start(s32[256]{0:T(256)} %param.11), channel_id=1, source_target_pairs={{0,64},{8,72},{16,80},{24,88},{32,96},{40,104},{48,112},{56,120},{... | collective-permute-start | bytes 3080 | tf_op jit(solution)/shard_map/ppermute | solution.py:16
  18.1 3.7 %collective-permute-start.9 = (s32[256]{0:T(256)}, s32[256]{0:T(256)S(1)}, u32[]{:S(2)}, u32[]{:S(2)}) collective-permute-start(s32[256]{0:T(256)} %param.11), channel_id=1, source_target_pairs={{0,56},{8,64},{16,72},{24,80},{32,88},{40,96},{48,104},{56,112},{6... | collective-permute-start | bytes 3080 | tf_op jit(solution)/shard_map/ppermute | solution.py:16
  21.8 4.3 %collective-permute-start.10 = (s32[256]{0:T(256)}, s32[256]{0:T(256)S(1)}, u32[]{:S(2)}, u32[]{:S(2)}) collective-permute-start(s32[256]{0:T(256)} %param.11), channel_id=1, source_target_pairs={{0,48},{8,56},{16,64},{24,72},{32,80},{40,88},{48,96},{56,104},{64... | collective-permute-start | bytes 3080 | tf_op jit(solution)/shard_map/ppermute | solution.py:16
  26.1 6.4 %collective-permute-start.11 = (s32[256]{0:T(256)}, s32[256]{0:T(256)S(1)}, u32[]{:S(2)}, u32[]{:S(2)}) collective-permute-start(s32[256]{0:T(256)} %param.11), channel_id=1, source_target_pairs={{0,40},{8,48},{16,56},{24,64},{32,72},{40,80},{48,88},{56,96},{64,... | collective-permute-start | bytes 3080 | tf_op jit(solution)/shard_map/ppermute | solution.py:16
  32.5 4.3 %collective-permute-start.12 = (s32[256]{0:T(256)}, s32[256]{0:T(256)S(1)}, u32[]{:S(2)}, u32[]{:S(2)}) collective-permute-start(s32[256]{0:T(256)} %param.11), channel_id=1, source_target_pairs={{0,32},{8,40},{16,48},{24,56},{32,64},{40,72},{48,80},{56,88},{64,... | collective-permute-start | bytes 3080 | tf_op jit(solution)/shard_map/ppermute | solution.py:16
  36.9 3.5 collective-permute-start.13
  40.4 2.8 collective-permute-start.14
  43.2 3.4 collective-permute-start.15
  46.8 1.5 collective-permute-done.15
  49.0 1.3 convert_reduce_fusion.2
  50.8 1.4 compare_and_fusion.1
  52.2 4.4 %all-gather.4.cloned.1.call-done = bf16[256,2048]{1,0:T(8,128)(2,1)} async-done(((bf16[256,256]{1,0:T(8,128)(2,1)}), bf16[256,2048]{1,0:T(8,128)(2,1)}) %all-gather.4.cloned.1.call-update) | async-done | bytes 1048592 | tf_op jit(solution)/shard_map/all_gather | solution.py:73
  56.7 1.5 convert_reduce_fusion.1
  58.2 1.6 fusion.12
  59.9 90.5 %all-gather.6.cloned.1.call-done = bf16[2048,2560]{1,0:T(8,128)(2,1)} async-done(((bf16[32,2560]{1,0:T(8,128)(2,1)}), bf16[2048,2560]{1,0:T(8,128)(2,1)}) %all-gather.6.cloned.1.call-update) | async-done | bytes 10485776 | tf_op jit(solution)/shard_map/all_gather | solution.py:56
  150.4 1.9 fusion.29
  152.8 3.4 collective-permute-start.16
  156.2 2.5 collective-permute-start.17
  158.7 4.2 %collective-permute-start.18 = (bf16[256,2,128]{2,0,1:T(8,128)(2,1)S(1)}, bf16[256,2,128]{2,0,1:T(8,128)(2,1)S(1)}, u32[]{:S(2)}, u32[]{:S(2)}) collective-permute-start(bf16[256,2,128]{2,0,1:T(8,128)(2,1)S(1)} %maximum_convert_fusion), channel_id=1, source_target_pairs={{0,48},{8,56},{16,64},{24,72},{32,80},{40,88},{48,96},{56,104},{64... | collective-permute-start | bytes 393224 | tf_op jit(solution)/shard_map/ppermute | solution.py:16
  163.0 4.1 %collective-permute-start.19 = (bf16[256,2,128]{2,0,1:T(8,128)(2,1)S(1)}, bf16[256,2,128]{2,0,1:T(8,128)(2,1)S(1)}, u32[]{:S(2)}, u32[]{:S(2)}) collective-permute-start(bf16[256,2,128]{2,0,1:T(8,128)(2,1)S(1)} %maximum_convert_fusion), channel_id=1, source_target_pairs={{0,40},{8,48},{16,56},{24,64},{32,72},{40,80},{48,88},{56,96},{64,... | collective-permute-start | bytes 393224 | tf_op jit(solution)/shard_map/ppermute | solution.py:16
  167.0 2.8 collective-permute-start.20
  169.8 1.9 fusion.31
  172.0 1.7 convolution_convert_fusion.2
  173.9 3.6 collective-permute-start.21
  177.5 3.5 collective-permute-start.22
  181.1 3.0 collective-permute-start.23
  184.2 2.4 collective-permute-start
  186.6 3.4 collective-permute-start.1
  190.1 3.2 collective-permute-start.2
  193.3 2.2 collective-permute-start.3
  195.6 3.6 collective-permute-start.4
  200.2 3.5 collective-permute-start.5
  203.8 2.3 collective-permute-start.6
  206.1 3.5 collective-permute-start.7
  209.8 1.8 collective-permute-done.6
  213.8 4.7 %fusion.62 = (f32[2,256]{1,0:T(2,128)S(1)}, f32[2,256,2304]{2,1,0:T(8,128)}) fusion(bf16[2304,2,128]{2,0,1:T(8,128)(2,1)S(1)} %copy-done.7, pred[256,2304]{1,0:T(8,128)(4,1)S(1)} %compare_and_fusion.1, bf16[256,2,64]{2,0,1:T(8,128)(2,1)S(1)} %get-tuple-element.3, bf16[256,2,64]{2,0,1:T(8,128)(2,1)S(1)} %get-tuple-element.2), kind=kOutput, calls=%fused_computation.111 | convolution fusion | flops 308152576 | bytes 6621184 | tf_op jit(solution)/shard_map/sub | solution.py:98
  218.5 3.7 %fusion.27 = bf16[2,128,256]{2,1,0:T(8,128)(2,1)S(1)} fusion(bf16[2304,2,128]{0,2,1:T(8,128)(2,1)} %copy-done.8, f32[2,256,2304]{2,1,0:T(8,128)} %get-tuple-element.13, f32[2,256]{1,0:T(2,128)S(1)} %get-tuple-element.12), kind=kOutput, calls=%fused_computation.35 | convolution fusion | flops 304414720 | bytes 6031360 | tf_op jit(solution)/shard_map/hqk,khd->qhd/dot_general | solution.py:100
  222.2 2.8 convolution_convert_fusion.1
  225.0 37.6 %reduce-scatter.3.cloned.1.call-done = bf16[256,256]{1,0:T(8,128)(2,1)} async-done(((bf16[256,2048]{1,0:T(8,128)(2,1)}), bf16[256,256]{1,0:T(8,128)(2,1)}) %reduce-scatter.3.cloned.1.call-update) | async-done | bytes 131088 | tf_op jit(solution)/shard_map/reduce_scatter | solution.py:105
  262.6 1.6 add_convert_fusion.1
  264.4 42.0 %all-gather.8.cloned.1.call-done = bf16[256,2048]{1,0:T(8,128)(2,1)} async-done(((bf16[256,256]{1,0:T(8,128)(2,1)}), bf16[256,2048]{1,0:T(8,128)(2,1)}) %all-gather.8.cloned.1.call-update) | async-done | bytes 1048592 | tf_op jit(solution)/shard_map/all_gather | solution.py:109
  306.4 1.5 convert_reduce_fusion
  307.9 1.6 fusion.10
  309.6 2.3 fusion.17
  312.0 4.7 %convolution_convert_fusion = bf16[256,2048]{1,0:T(8,128)(2,1)} fusion(bf16[2048,2560]{1,0:T(8,128)(2,1)} %all-gather.6.cloned.1.call-done, f32[256,512]{1,0:T(8,128)S(1)} %fusion.17, bf16[256,2048]{1,0:T(8,128)(2,1)S(1)} %copy-done.1, f32[256]{0:T(256)S(1)} %add_rsqrt_fusion, f32[256]{0:T(256)S(1)} %broadcast_multiply_fusion), kind=kOutput, calls=%fused_computation.14 | convolution fusion | flops 1077149696 | bytes 6817792 | tf_op jit(solution)/shard_map/dot_general | solution.py:114
  317.0 1.2 scatter_fusion
  318.2 39.1 %reduce-scatter.5.cloned.1.call-done = bf16[256,256]{1,0:T(8,128)(2,1)} async-done(((bf16[256,2048]{1,0:T(8,128)(2,1)}), bf16[256,256]{1,0:T(8,128)(2,1)}) %reduce-scatter.5.cloned.1.call-update) | async-done | bytes 131088 | tf_op jit(solution)/shard_map/reduce_scatter | solution.py:117
  357.3 1.6 add_convert_fusion
  (111 shorter events, 13.0 us)
Async XLA Ops:
  7.2 49.5 %all-gather.4.cloned.1.call-start = ((), (), s32[]{:S(2)}) async-start(), calls=%async_computation.2 | async-start | bytes 1179648 | tf_op jit(solution)/shard_map/all_gather | solution.py:73
  7.9 142.5 %all-gather.6.cloned.1.call-start = ((), (), s32[]{:S(2)}) async-start(), calls=%async_computation.3 | async-start | bytes 10649600 | tf_op jit(solution)/shard_map/all_gather | solution.py:56
  13.1 0.7 copy-start.5
  13.8 248.8 %reduce-scatter.3.cloned.1.call-start = ((), (), s32[]{:S(2)}) async-start(), calls=%async_computation.4 | async-start | bytes 1179648 | tf_op jit(solution)/shard_map/reduce_scatter | solution.py:105
  13.8 23.0 %collective-permute-start.8 = (s32[256]{0:T(256)}, s32[256]{0:T(256)S(1)}, u32[]{:S(2)}, u32[]{:S(2)}) collective-permute-start(s32[256]{0:T(256)} %param.11), channel_id=1, source_target_pairs={{0,64},{8,72},{16,80},{24,88},{32,96},{40,104},{48,112},{56,120},{... | collective-permute-start | bytes 3080 | tf_op jit(solution)/shard_map/ppermute | solution.py:16
  18.1 22.2 %collective-permute-start.9 = (s32[256]{0:T(256)}, s32[256]{0:T(256)S(1)}, u32[]{:S(2)}, u32[]{:S(2)}) collective-permute-start(s32[256]{0:T(256)} %param.11), channel_id=1, source_target_pairs={{0,56},{8,64},{16,72},{24,80},{32,88},{40,96},{48,104},{56,112},{6... | collective-permute-start | bytes 3080 | tf_op jit(solution)/shard_map/ppermute | solution.py:16
  21.8 21.3 %collective-permute-start.10 = (s32[256]{0:T(256)}, s32[256]{0:T(256)S(1)}, u32[]{:S(2)}, u32[]{:S(2)}) collective-permute-start(s32[256]{0:T(256)} %param.11), channel_id=1, source_target_pairs={{0,48},{8,56},{16,64},{24,72},{32,80},{40,88},{48,96},{56,104},{64... | collective-permute-start | bytes 3080 | tf_op jit(solution)/shard_map/ppermute | solution.py:16
  26.1 20.5 %collective-permute-start.11 = (s32[256]{0:T(256)}, s32[256]{0:T(256)S(1)}, u32[]{:S(2)}, u32[]{:S(2)}) collective-permute-start(s32[256]{0:T(256)} %param.11), channel_id=1, source_target_pairs={{0,40},{8,48},{16,56},{24,64},{32,72},{40,80},{48,88},{56,96},{64,... | collective-permute-start | bytes 3080 | tf_op jit(solution)/shard_map/ppermute | solution.py:16
  32.5 14.2 %collective-permute-start.12 = (s32[256]{0:T(256)}, s32[256]{0:T(256)S(1)}, u32[]{:S(2)}, u32[]{:S(2)}) collective-permute-start(s32[256]{0:T(256)} %param.11), channel_id=1, source_target_pairs={{0,32},{8,40},{16,48},{24,56},{32,64},{40,72},{48,80},{56,88},{64,... | collective-permute-start | bytes 3080 | tf_op jit(solution)/shard_map/ppermute | solution.py:16
  36.9 9.8 %collective-permute-start.13 = (s32[256]{0:T(256)}, s32[256]{0:T(256)S(1)}, u32[]{:S(2)}, u32[]{:S(2)}) collective-permute-start(s32[256]{0:T(256)} %param.11), channel_id=1, source_target_pairs={{0,24},{8,32},{16,40},{24,48},{32,56},{40,64},{48,72},{56,80},{64,... | collective-permute-start | bytes 3080 | tf_op jit(solution)/shard_map/ppermute | solution.py:16
  40.4 6.3 %collective-permute-start.14 = (s32[256]{0:T(256)}, s32[256]{0:T(256)S(1)}, u32[]{:S(2)}, u32[]{:S(2)}) collective-permute-start(s32[256]{0:T(256)} %param.11), channel_id=1, source_target_pairs={{0,16},{8,24},{16,32},{24,40},{32,48},{40,56},{48,64},{56,72},{64,... | collective-permute-start | bytes 3080 | tf_op jit(solution)/shard_map/ppermute | solution.py:16
  43.2 5.1 %collective-permute-start.15 = (s32[256]{0:T(256)}, s32[256]{0:T(256)S(1)}, u32[]{:S(2)}, u32[]{:S(2)}) collective-permute-start(s32[256]{0:T(256)} %param.11), channel_id=1, source_target_pairs={{0,8},{8,16},{16,24},{24,32},{32,40},{40,48},{48,56},{56,64},{64,7... | collective-permute-start | bytes 3080 | tf_op jit(solution)/shard_map/ppermute | solution.py:16
  56.7 93.7 %copy-start = (bf16[256,2048]{1,0:T(8,128)(2,1)S(1)}, bf16[256,2048]{1,0:T(8,128)(2,1)}, u32[]{:S(2)}) copy-start(bf16[256,2048]{1,0:T(8,128)(2,1)} %all-gather.4.cloned.1.call-done) | copy-start | bytes 3145732
  152.8 21.1 %collective-permute-start.16 = (bf16[256,2,128]{2,0,1:T(8,128)(2,1)S(1)}, bf16[256,2,128]{2,0,1:T(8,128)(2,1)S(1)}, u32[]{:S(2)}, u32[]{:S(2)}) collective-permute-start(bf16[256,2,128]{2,0,1:T(8,128)(2,1)S(1)} %maximum_convert_fusion), channel_id=1, source_target_pairs={{0,64},{8,72},{16,80},{24,88},{32,96},{40,104},{48,112},{56,120},{... | collective-permute-start | bytes 393224 | tf_op jit(solution)/shard_map/ppermute | solution.py:16
  156.2 21.3 %collective-permute-start.17 = (bf16[256,2,128]{2,0,1:T(8,128)(2,1)S(1)}, bf16[256,2,128]{2,0,1:T(8,128)(2,1)S(1)}, u32[]{:S(2)}, u32[]{:S(2)}) collective-permute-start(bf16[256,2,128]{2,0,1:T(8,128)(2,1)S(1)} %maximum_convert_fusion), channel_id=1, source_target_pairs={{0,56},{8,64},{16,72},{24,80},{32,88},{40,96},{48,104},{56,112},{6... | collective-permute-start | bytes 393224 | tf_op jit(solution)/shard_map/ppermute | solution.py:16
  158.7 22.3 %collective-permute-start.18 = (bf16[256,2,128]{2,0,1:T(8,128)(2,1)S(1)}, bf16[256,2,128]{2,0,1:T(8,128)(2,1)S(1)}, u32[]{:S(2)}, u32[]{:S(2)}) collective-permute-start(bf16[256,2,128]{2,0,1:T(8,128)(2,1)S(1)} %maximum_convert_fusion), channel_id=1, source_target_pairs={{0,48},{8,56},{16,64},{24,72},{32,80},{40,88},{48,96},{56,104},{64... | collective-permute-start | bytes 393224 | tf_op jit(solution)/shard_map/ppermute | solution.py:16
  163.0 21.2 %collective-permute-start.19 = (bf16[256,2,128]{2,0,1:T(8,128)(2,1)S(1)}, bf16[256,2,128]{2,0,1:T(8,128)(2,1)S(1)}, u32[]{:S(2)}, u32[]{:S(2)}) collective-permute-start(bf16[256,2,128]{2,0,1:T(8,128)(2,1)S(1)} %maximum_convert_fusion), channel_id=1, source_target_pairs={{0,40},{8,48},{16,56},{24,64},{32,72},{40,80},{48,88},{56,96},{64,... | collective-permute-start | bytes 393224 | tf_op jit(solution)/shard_map/ppermute | solution.py:16
  167.0 19.5 %collective-permute-start.20 = (bf16[256,2,128]{2,0,1:T(8,128)(2,1)S(1)}, bf16[256,2,128]{2,0,1:T(8,128)(2,1)S(1)}, u32[]{:S(2)}, u32[]{:S(2)}) collective-permute-start(bf16[256,2,128]{2,0,1:T(8,128)(2,1)S(1)} %maximum_convert_fusion), channel_id=1, source_target_pairs={{0,32},{8,40},{16,48},{24,56},{32,64},{40,72},{48,80},{56,88},{64,... | collective-permute-start | bytes 393224 | tf_op jit(solution)/shard_map/ppermute | solution.py:16
  173.9 16.1 %collective-permute-start.21 = (bf16[256,2,128]{2,0,1:T(8,128)(2,1)S(1)}, bf16[256,2,128]{2,0,1:T(8,128)(2,1)S(1)}, u32[]{:S(2)}, u32[]{:S(2)}) collective-permute-start(bf16[256,2,128]{2,0,1:T(8,128)(2,1)S(1)} %maximum_convert_fusion), channel_id=1, source_target_pairs={{0,24},{8,32},{16,40},{24,48},{32,56},{40,64},{48,72},{56,80},{64,... | collective-permute-start | bytes 393224 | tf_op jit(solution)/shard_map/ppermute | solution.py:16
  177.5 15.7 %collective-permute-start.22 = (bf16[256,2,128]{2,0,1:T(8,128)(2,1)S(1)}, bf16[256,2,128]{2,0,1:T(8,128)(2,1)S(1)}, u32[]{:S(2)}, u32[]{:S(2)}) collective-permute-start(bf16[256,2,128]{2,0,1:T(8,128)(2,1)S(1)} %maximum_convert_fusion), channel_id=1, source_target_pairs={{0,16},{8,24},{16,32},{24,40},{32,48},{40,56},{48,64},{56,72},{64,... | collective-permute-start | bytes 393224 | tf_op jit(solution)/shard_map/ppermute | solution.py:16
  181.1 14.5 %collective-permute-start.23 = (bf16[256,2,128]{2,0,1:T(8,128)(2,1)S(1)}, bf16[256,2,128]{2,0,1:T(8,128)(2,1)S(1)}, u32[]{:S(2)}, u32[]{:S(2)}) collective-permute-start(bf16[256,2,128]{2,0,1:T(8,128)(2,1)S(1)} %maximum_convert_fusion), channel_id=1, source_target_pairs={{0,8},{8,16},{16,24},{24,32},{32,40},{40,48},{48,56},{56,64},{64,7... | collective-permute-start | bytes 393224 | tf_op jit(solution)/shard_map/ppermute | solution.py:16
  184.2 16.1 %collective-permute-start = (bf16[256,2,128]{0,2,1:T(8,128)(2,1)S(1)}, bf16[256,2,128]{0,2,1:T(8,128)(2,1)S(1)}, u32[]{:S(2)}, u32[]{:S(2)}) collective-permute-start(bf16[256,2,128]{0,2,1:T(8,128)(2,1)S(1)} %bitcast.16), channel_id=1, source_target_pairs={{0,64},{8,72},{16,80},{24,88},{32,96},{40,104},{48,112},{56,120},{... | collective-permute-start | bytes 393224 | tf_op jit(solution)/shard_map/ppermute | solution.py:16
  186.6 17.2 %collective-permute-start.1 = (bf16[256,2,128]{0,2,1:T(8,128)(2,1)S(1)}, bf16[256,2,128]{0,2,1:T(8,128)(2,1)S(1)}, u32[]{:S(2)}, u32[]{:S(2)}) collective-permute-start(bf16[256,2,128]{0,2,1:T(8,128)(2,1)S(1)} %bitcast.17), channel_id=1, source_target_pairs={{0,56},{8,64},{16,72},{24,80},{32,88},{40,96},{48,104},{56,112},{6... | collective-permute-start | bytes 393224 | tf_op jit(solution)/shard_map/ppermute | solution.py:16
  190.1 16.0 %collective-permute-start.2 = (bf16[256,2,128]{0,2,1:T(8,128)(2,1)S(1)}, bf16[256,2,128]{0,2,1:T(8,128)(2,1)S(1)}, u32[]{:S(2)}, u32[]{:S(2)}) collective-permute-start(bf16[256,2,128]{0,2,1:T(8,128)(2,1)S(1)} %bitcast.18), channel_id=1, source_target_pairs={{0,48},{8,56},{16,64},{24,72},{32,80},{40,88},{48,96},{56,104},{64... | collective-permute-start | bytes 393224 | tf_op jit(solution)/shard_map/ppermute | solution.py:16
  193.3 16.4 %collective-permute-start.3 = (bf16[256,2,128]{0,2,1:T(8,128)(2,1)S(1)}, bf16[256,2,128]{0,2,1:T(8,128)(2,1)S(1)}, u32[]{:S(2)}, u32[]{:S(2)}) collective-permute-start(bf16[256,2,128]{0,2,1:T(8,128)(2,1)S(1)} %bitcast.19), channel_id=1, source_target_pairs={{0,40},{8,48},{16,56},{24,64},{32,72},{40,80},{48,88},{56,96},{64,... | collective-permute-start | bytes 393224 | tf_op jit(solution)/shard_map/ppermute | solution.py:16
  195.6 14.2 %collective-permute-start.4 = (bf16[256,2,128]{0,2,1:T(8,128)(2,1)S(1)}, bf16[256,2,128]{0,2,1:T(8,128)(2,1)S(1)}, u32[]{:S(2)}, u32[]{:S(2)}) collective-permute-start(bf16[256,2,128]{0,2,1:T(8,128)(2,1)S(1)} %bitcast.20), channel_id=1, source_target_pairs={{0,32},{8,40},{16,48},{24,56},{32,64},{40,72},{48,80},{56,88},{64,... | collective-permute-start | bytes 393224 | tf_op jit(solution)/shard_map/ppermute | solution.py:16
  199.2 1.0 copy-start.6
  200.2 13.6 %copy-start.7 = (bf16[2304,2,128]{2,0,1:T(8,128)(2,1)S(1)}, bf16[2304,2,128]{2,0,1:T(8,128)(2,1)}, u32[]{:S(2)}) copy-start(bf16[2304,2,128]{2,0,1:T(8,128)(2,1)} %copy-done.6) | copy-start | bytes 3538948
  200.2 9.5 %collective-permute-start.5 = (bf16[256,2,128]{0,2,1:T(8,128)(2,1)S(1)}, bf16[256,2,128]{0,2,1:T(8,128)(2,1)S(1)}, u32[]{:S(2)}, u32[]{:S(2)}) collective-permute-start(bf16[256,2,128]{0,2,1:T(8,128)(2,1)S(1)} %bitcast.21), channel_id=1, source_target_pairs={{0,24},{8,32},{16,40},{24,48},{32,56},{40,64},{48,72},{56,80},{64,... | collective-permute-start | bytes 393224 | tf_op jit(solution)/shard_map/ppermute | solution.py:16
  203.8 7.8 %collective-permute-start.6 = (bf16[256,2,128]{0,2,1:T(8,128)(2,1)S(1)}, bf16[256,2,128]{0,2,1:T(8,128)(2,1)S(1)}, u32[]{:S(2)}, u32[]{:S(2)}) collective-permute-start(bf16[256,2,128]{0,2,1:T(8,128)(2,1)S(1)} %bitcast.22), channel_id=1, source_target_pairs={{0,16},{8,24},{16,32},{24,40},{32,48},{40,56},{48,64},{56,72},{64,... | collective-permute-start | bytes 393224 | tf_op jit(solution)/shard_map/ppermute | solution.py:16
  206.1 6.6 %collective-permute-start.7 = (bf16[256,2,128]{0,2,1:T(8,128)(2,1)S(1)}, bf16[256,2,128]{0,2,1:T(8,128)(2,1)S(1)}, u32[]{:S(2)}, u32[]{:S(2)}) collective-permute-start(bf16[256,2,128]{0,2,1:T(8,128)(2,1)S(1)} %bitcast.23), channel_id=1, source_target_pairs={{0,8},{8,16},{16,24},{24,32},{32,40},{40,48},{48,56},{56,64},{64,7... | collective-permute-start | bytes 393224 | tf_op jit(solution)/shard_map/ppermute | solution.py:16
  212.7 1.0 copy-start.8
  222.2 40.4 %copy-start.4 = (bf16[256,256]{1,0:T(8,128)(2,1)S(1)}, bf16[256,256]{1,0:T(8,128)(2,1)}, u32[]{:S(2)}) copy-start(bf16[256,256]{1,0:T(8,128)(2,1)} %param.10) | copy-start | bytes 393220
  225.0 81.4 %all-gather.8.cloned.1.call-start = ((), (), s32[]{:S(2)}) async-start(), calls=%async_computation.5 | async-start | bytes 1179648 | tf_op jit(solution)/shard_map/all_gather | solution.py:109
  264.2 93.1 %reduce-scatter.5.cloned.1.call-start = ((), (), s32[]{:S(2)}) async-start(), calls=%async_computation.6 | async-start | bytes 1179648 | tf_op jit(solution)/shard_map/reduce_scatter | solution.py:117
  306.4 3.2 copy-start.1
  311.9 4.7 %copy-start.9 = (s32[16]{0:T(128)S(1)}, s32[16]{0:T(128)}, u32[]{:S(2)}) copy-start(s32[16]{0:T(128)} %param.12) | copy-start | bytes 196
  316.6 40.7 %copy-start.2 = (bf16[256,256]{1,0:T(8,128)(2,1)S(1)}, bf16[256,256]{1,0:T(8,128)(2,1)}, u32[]{:S(2)}) copy-start(bf16[256,256]{1,0:T(8,128)(2,1)} %add_convert_fusion.1) | copy-start | bytes 393220
  318.2 40.7 %copy-start.3 = (bf16[2,16,16,256]{3,2,1,0:T(8,128)(2,1)}, bf16[2,16,16,256]{3,2,1,0:T(8,128)(2,1)S(1)}, u32[]{:S(2)}) copy-start(bf16[2,16,16,256]{3,2,1,0:T(8,128)(2,1)S(1)} %scatter_fusion) | copy-start | bytes 786436
Sparse Core Ops, SparseCore 0:
  10.0 46.6 all-gather.3
  60.6 89.7 all-gather.5
  225.1 37.4 reduce-scatter.2
  265.0 41.3 all-gather.7
  316.8 40.5 reduce-scatter.4
where the time goes:
time: 367 us; the launch traced here: 365 us
  waiting for transfers between devices  219 us (60%)
  starting transfers between devices  84.2 us (23%)
  matrix products  23.6 us (6%)
  between operations  14.6 us (4%)
  other arithmetic  13.2 us (4%)
  local copies, waits for them, and re-layouts  11 us (3%)
    all_gather x1, waiting for transfers between devices, per_device(): lax.all_gather(jnp.concatenate(pieces, axis=1), 'wide', axis=0, tiled=True)  90.5 us
    ppermute x24, starting transfers between devices, shifted(): lax.ppermute(value, axis, [(source, source + steps) for source in range(f...  83.8 us
    all_gather x1, waiting for transfers between devices, per_device(): whole_two = lax.all_gather(first_res, 'narrow', axis=1, tiled=True)  42 us
    reduce_scatter x1, waiting for transfers between devices, per_device(): lax.psum_scatter(down_terms.astype(jnp.bfloat16), 'narrow', scatter_dimen...  39.1 us
    reduce_scatter x1, waiting for transfers between devices, per_device(): lax.psum_scatter(attn_terms.astype(jnp.bfloat16), 'narrow', scatter_dimen...  37.6 us
    unnamed x46, local copies, waits for them, and re-layouts  7.88 us
    dot_general x4, matrix products, add_rows(): return jnp.dot(source, piece, preferred_element_type=jnp.float32)  7.84 us
  transfers between devices with their start and end apart: 29, of which 8 were waited for; matrix products, arithmetic and copies ran while one was open for 5% of the time, Pallas kernels for 0%

commit v1 on v0

--- a/solution.py
+++ b/solution.py
@@ -2,6 +2,7 @@
 import jax.numpy as jnp
 from jax import lax
 from jax.sharding import PartitionSpec as P
+from jax.lax import all_to_all, psum
 
 HEAD_DIM = 128
 REACH = 8
@@ -53,7 +54,15 @@
     ff_width = wg.shape[1]
     pieces = [wq, wk, wv, wo.T, wg, wu, wd.T]
     widths = [piece.shape[1] for piece in pieces]
-    gathered = lax.all_gather(jnp.concatenate(pieces, axis=1), "wide", axis=0, tiled=True)
+    gathered = jnp.concatenate(
+        all_to_all(
+            jnp.stack([jnp.concatenate(pieces, axis=1)] * psum(1, axis_name="wide")),
+            axis_name="wide",
+            split_axis=0,
+            concat_axis=0,
+        ),
+        axis=0,
+    )
     offsets = [sum(widths[:k]) for k in range(len(widths))]
     full = [gathered[:, o : o + w] for o, w in zip(offsets, widths)]
     wq_all, wk_all, wv_all, wo_t, wg_all, wu_all, wd_t = full

time: 367 us -> 494 us (1.35)
  waiting for transfers between devices: 219 us -> 328 us
  starting transfers between devices: 84.2 us -> 99.2 us
    ppermute x24, waiting for transfers between devices: 4.52 us -> 208 us  [shifted(): lax.ppermute(value, axis, [(source, source + steps) for source in range(f...]
    all_gather x1 -> x0, waiting for transfers between devices: 90.5 us -> none  [per_device(): lax.all_gather(jnp.concatenate(pieces, axis=1), 'wide', axis=0, tiled=True)]
    all_to_all x0 -> x1, starting transfers between devices: none -> 14.1 us  [per_device(): all_to_all(jnp.stack([jnp.concatenate(pieces, axis=1)] * psum(1, axis_nam...]
    another operation x0 -> x1, local copies, waits for them, and re-layouts: none -> 5.11 us  [per_device(): jnp.stack([jnp.concatenate(pieces, axis=1)] * psum(1, axis_name='wide'))]
  transfers between devices with their start and end apart: 29 -> 29, of which waited for: 8 -> 7; matrix products, arithmetic and copies ran while one was open for 5% -> 2% of each run, Pallas kernels for 0% -> 0%
where the time goes in v1:
time: 494 us; the launch traced here: 492 us
  waiting for transfers between devices  328 us (66%)
  starting transfers between devices  99.2 us (20%)
  matrix products  24.6 us (5%)
  between operations  14.7 us (3%)
  local copies, waits for them, and re-layouts  13.7 us (3%)
  other arithmetic  11.9 us (2%)
    ppermute x24, waiting for transfers between devices, shifted(): lax.ppermute(value, axis, [(source, source + steps) for source in range(f...  208 us
    ppermute x24, starting transfers between devices, shifted(): lax.ppermute(value, axis, [(source, source + steps) for source in range(f...  84.9 us
    all_gather x1, waiting for transfers between devices, per_device(): whole_two = lax.all_gather(first_res, 'narrow', axis=1, tiled=True)  42.3 us
    reduce_scatter x1, waiting for transfers between devices, per_device(): lax.psum_scatter(down_terms.astype(jnp.bfloat16), 'narrow', scatter_dimen...  39 us
    reduce_scatter x1, waiting for transfers between devices, per_device(): lax.psum_scatter(attn_terms.astype(jnp.bfloat16), 'narrow', scatter_dimen...  38.2 us
    all_to_all x1, starting transfers between devices, per_device(): all_to_all(jnp.stack([jnp.concatenate(pieces, axis=1)] * psum(1, axis_nam...  14.1 us
  transfers between devices with their start and end apart: 29, of which 7 were waited for; matrix products, arithmetic and copies ran while one was open for 2% of the time, Pallas kernels for 0%

profile of v1, /device:TPU:6, one launch (start us, length us, event | category | flops | bytes accessed | tf_op | source)
XLA Modules:
  0.0 492.0 jit_solution(3044305114060533244)
XLA Ops:
  12.3 5.1 %stack.4 = bf16[64,32,2560]{2,1,0:T(8,128)(2,1)} broadcast(bf16[32,2560]{1,0:T(8,128)(2,1)S(1)} %constant_dynamic-update-slice_fusion), dimensions={1,2} | broadcast | bytes 10649600 | tf_op jit(solution)/shard_map/stack | solution.py:59
  17.4 14.1 %all-to-all-start = ((bf16[64,32,2560]{2,1,0:T(8,128)(2,1)}), bf16[64,32,2560]{2,1,0:T(8,128)(2,1)}, u32[]{:S(2)}, u32[]{:S(2)}) async-start(bf16[64,32,2560]{2,1,0:T(8,128)(2,1)} %stack.4), calls=%async_computation | async-start | bytes 20971520 | tf_op jit(solution)/shard_map/all_to_all | solution.py:58
  31.6 3.4 collective-permute-start.8
  35.0 3.1 collective-permute-start.9
  38.1 3.4 collective-permute-start.10
  41.6 5.2 %collective-permute-start.11 = (s32[256]{0:T(256)S(1)}, s32[256]{0:T(256)S(1)}, u32[]{:S(2)}, u32[]{:S(2)}) collective-permute-start(s32[256]{0:T(256)S(1)} %copy-done.8), channel_id=1, source_target_pairs={{0,40},{8,48},{16,56},{24,64},{32,72},{40,80},{48,88},{56,96},{64,... | collective-permute-start | bytes 3080 | tf_op jit(solution)/shard_map/ppermute | solution.py:17
  46.8 4.3 collective-permute-start.12
  51.2 203.2 %collective-permute-done.8 = s32[256]{0:T(256)S(1)} collective-permute-done((s32[256]{0:T(256)S(1)}, s32[256]{0:T(256)S(1)}, u32[]{:S(2)}, u32[]{:S(2)}) %collective-permute-start.8) | collective-permute-done | bytes 1056 | tf_op jit(solution)/shard_map/ppermute | solution.py:17
  254.4 2.8 collective-permute-start.13
  257.2 6.9 %collective-permute-start.14 = (s32[256]{0:T(256)S(1)}, s32[256]{0:T(256)S(1)}, u32[]{:S(2)}, u32[]{:S(2)}) collective-permute-start(s32[256]{0:T(256)S(1)} %copy-done.8), channel_id=1, source_target_pairs={{0,16},{8,24},{16,32},{24,40},{32,48},{40,56},{48,64},{56,72},{64,... | collective-permute-start | bytes 3080 | tf_op jit(solution)/shard_map/ppermute | solution.py:17
  264.1 3.1 collective-permute-start.15
  267.4 2.5 collective-permute-done.15
  271.8 1.5 convert_reduce_fusion.1
  273.4 1.6 fusion.12
  275.1 1.7 convolution_convert_fusion.2
  276.9 4.5 collective-permute-start
  281.3 1.3 collective-permute-start.1
  282.7 3.2 collective-permute-start.2
  285.9 7.4 %collective-permute-start.3 = (bf16[256,2,128]{0,2,1:T(8,128)(2,1)S(1)}, bf16[256,2,128]{0,2,1:T(8,128)(2,1)S(1)}, u32[]{:S(2)}, u32[]{:S(2)}) collective-permute-start(bf16[256,2,128]{0,2,1:T(8,128)(2,1)S(1)} %bitcast.20), channel_id=1, source_target_pairs={{0,40},{8,48},{16,56},{24,64},{32,72},{40,80},{48,88},{56,96},{64,... | collective-permute-start | bytes 393224 | tf_op jit(solution)/shard_map/ppermute | solution.py:17
  293.3 2.3 collective-permute-start.4
  295.5 1.9 fusion.29
  297.7 1.9 fusion.31
  300.2 3.6 collective-permute-start.5
  303.9 2.8 collective-permute-start.6
  306.7 3.1 collective-permute-start.7
  309.8 2.3 collective-permute-start.16
  312.1 4.3 collective-permute-start.17
  316.5 2.8 collective-permute-start.18
  319.3 1.9 collective-permute-start.19
  321.3 4.3 collective-permute-start.20
  325.7 2.8 collective-permute-start.21
  328.5 2.8 collective-permute-start.22
  331.3 3.4 collective-permute-start.23
  334.9 1.3 collective-permute-done.22
  336.2 1.4 collective-permute-done.23
  338.7 6.0 %fusion.62 = (f32[2,256]{1,0:T(2,128)S(1)}, f32[2,256,2304]{2,1,0:T(8,128)}) fusion(bf16[2304,2,128]{2,0,1:T(8,128)(2,1)} %copy-done.7, pred[256,2304]{1,0:T(8,128)(4,1)S(1)} %compare_and_fusion.1, bf16[256,2,64]{2,0,1:T(8,128)(2,1)S(1)} %get-tuple-element.3, bf16[256,2,64]{2,0,1:T(8,128)(2,1)S(1)} %get-tuple-element.2), kind=kOutput, calls=%fused_computation.111 | convolution fusion | flops 308152576 | bytes 6621184 | tf_op jit(solution)/shard_map/sub | solution.py:107
  344.7 3.3 fusion.27
  348.1 2.8 convolution_convert_fusion.1
  350.9 38.2 %reduce-scatter.3.cloned.1.call-done = bf16[256,256]{1,0:T(8,128)(2,1)} async-done(((bf16[256,2048]{1,0:T(8,128)(2,1)}), bf16[256,256]{1,0:T(8,128)(2,1)}) %reduce-scatter.3.cloned.1.call-update) | async-done | bytes 131088 | tf_op jit(solution)/shard_map/reduce_scatter | solution.py:114
  389.1 1.6 add_convert_fusion.1
  390.8 42.3 %all-gather.5.cloned.1.call-done = bf16[256,2048]{1,0:T(8,128)(2,1)} async-done(((bf16[256,256]{1,0:T(8,128)(2,1)}), bf16[256,2048]{1,0:T(8,128)(2,1)}) %all-gather.5.cloned.1.call-update) | async-done | bytes 1048592 | tf_op jit(solution)/shard_map/all_gather | solution.py:118
  433.1 1.5 convert_reduce_fusion
  434.6 1.6 fusion.10
  436.3 2.3 fusion.17
  438.7 4.7 convolution_convert_fusion
  443.7 1.2 scatter_fusion
  444.9 39.0 %reduce-scatter.5.cloned.1.call-done = bf16[256,256]{1,0:T(8,128)(2,1)} async-done(((bf16[256,2048]{1,0:T(8,128)(2,1)}), bf16[256,256]{1,0:T(8,128)(2,1)}) %reduce-scatter.5.cloned.1.call-update) | async-done | bytes 131088 | tf_op jit(solution)/shard_map/reduce_scatter | solution.py:126
  483.9 1.6 add_convert_fusion
  (111 shorter events, 10.0 us)
Async XLA Ops:
  17.4 14.2 %copy-start.8 = (s32[256]{0:T(256)S(1)}, s32[256]{0:T(256)}, u32[]{:S(2)}) copy-start(s32[256]{0:T(256)} %param.11) | copy-start | bytes 3076
  17.4 257.6 %all-to-all-start = ((bf16[64,32,2560]{2,1,0:T(8,128)(2,1)}), bf16[64,32,2560]{2,1,0:T(8,128)(2,1)}, u32[]{:S(2)}, u32[]{:S(2)}) async-start(bf16[64,32,2560]{2,1,0:T(8,128)(2,1)} %stack.4), calls=%async_computation | async-start | bytes 20971520 | tf_op jit(solution)/shard_map/all_to_all | solution.py:58
  31.6 240.3 %all-gather.3.cloned.1.call-start = ((), (), s32[]{:S(2)}) async-start(), calls=%async_computation.3 | async-start | bytes 1179648 | tf_op jit(solution)/shard_map/all_gather | solution.py:82
  31.6 222.8 %collective-permute-start.8 = (s32[256]{0:T(256)S(1)}, s32[256]{0:T(256)S(1)}, u32[]{:S(2)}, u32[]{:S(2)}) collective-permute-start(s32[256]{0:T(256)S(1)} %copy-done.8), channel_id=1, source_target_pairs={{0,64},{8,72},{16,80},{24,88},{32,96},{40,104},{48,112},{56,120},{... | collective-permute-start | bytes 3080 | tf_op jit(solution)/shard_map/ppermute | solution.py:17
  35.0 222.2 %collective-permute-start.9 = (s32[256]{0:T(256)S(1)}, s32[256]{0:T(256)S(1)}, u32[]{:S(2)}, u32[]{:S(2)}) collective-permute-start(s32[256]{0:T(256)S(1)} %copy-done.8), channel_id=1, source_target_pairs={{0,56},{8,64},{16,72},{24,80},{32,88},{40,96},{48,104},{56,112},{6... | collective-permute-start | bytes 3080 | tf_op jit(solution)/shard_map/ppermute | solution.py:17
  38.1 226.0 %collective-permute-start.10 = (s32[256]{0:T(256)S(1)}, s32[256]{0:T(256)S(1)}, u32[]{:S(2)}, u32[]{:S(2)}) collective-permute-start(s32[256]{0:T(256)S(1)} %copy-done.8), channel_id=1, source_target_pairs={{0,48},{8,56},{16,64},{24,72},{32,80},{40,88},{48,96},{56,104},{64... | collective-permute-start | bytes 3080 | tf_op jit(solution)/shard_map/ppermute | solution.py:17
  41.6 225.7 %collective-permute-start.11 = (s32[256]{0:T(256)S(1)}, s32[256]{0:T(256)S(1)}, u32[]{:S(2)}, u32[]{:S(2)}) collective-permute-start(s32[256]{0:T(256)S(1)} %copy-done.8), channel_id=1, source_target_pairs={{0,40},{8,48},{16,56},{24,64},{32,72},{40,80},{48,88},{56,96},{64,... | collective-permute-start | bytes 3080 | tf_op jit(solution)/shard_map/ppermute | solution.py:17
  46.8 220.5 %collective-permute-start.12 = (s32[256]{0:T(256)S(1)}, s32[256]{0:T(256)S(1)}, u32[]{:S(2)}, u32[]{:S(2)}) collective-permute-start(s32[256]{0:T(256)S(1)} %copy-done.8), channel_id=1, source_target_pairs={{0,32},{8,40},{16,48},{24,56},{32,64},{40,72},{48,80},{56,88},{64,... | collective-permute-start | bytes 3080 | tf_op jit(solution)/shard_map/ppermute | solution.py:17
  51.1 338.0 %reduce-scatter.3.cloned.1.call-start = ((), (), s32[]{:S(2)}) async-start(), calls=%async_computation.4 | async-start | bytes 1179648 | tf_op jit(solution)/shard_map/reduce_scatter | solution.py:114
  254.4 12.9 %collective-permute-start.13 = (s32[256]{0:T(256)S(1)}, s32[256]{0:T(256)S(1)}, u32[]{:S(2)}, u32[]{:S(2)}) collective-permute-start(s32[256]{0:T(256)S(1)} %copy-done.8), channel_id=1, source_target_pairs={{0,24},{8,32},{16,40},{24,48},{32,56},{40,64},{48,72},{56,80},{64,... | collective-permute-start | bytes 3080 | tf_op jit(solution)/shard_map/ppermute | solution.py:17
  257.2 10.1 %collective-permute-start.14 = (s32[256]{0:T(256)S(1)}, s32[256]{0:T(256)S(1)}, u32[]{:S(2)}, u32[]{:S(2)}) collective-permute-start(s32[256]{0:T(256)S(1)} %copy-done.8), channel_id=1, source_target_pairs={{0,16},{8,24},{16,32},{24,40},{32,48},{40,56},{48,64},{56,72},{64,... | collective-permute-start | bytes 3080 | tf_op jit(solution)/shard_map/ppermute | solution.py:17
  264.1 5.7 %collective-permute-start.15 = (s32[256]{0:T(256)S(1)}, s32[256]{0:T(256)S(1)}, u32[]{:S(2)}, u32[]{:S(2)}) collective-permute-start(s32[256]{0:T(256)S(1)} %copy-done.8), channel_id=1, source_target_pairs={{0,8},{8,16},{16,24},{24,32},{32,40},{40,48},{48,56},{56,64},{64,7... | collective-permute-start | bytes 3080 | tf_op jit(solution)/shard_map/ppermute | solution.py:17
  271.8 3.2 copy-start
  276.9 23.3 %collective-permute-start = (bf16[256,2,128]{0,2,1:T(8,128)(2,1)S(1)}, bf16[256,2,128]{0,2,1:T(8,128)(2,1)S(1)}, u32[]{:S(2)}, u32[]{:S(2)}) collective-permute-start(bf16[256,2,128]{0,2,1:T(8,128)(2,1)S(1)} %bitcast.17), channel_id=1, source_target_pairs={{0,64},{8,72},{16,80},{24,88},{32,96},{40,104},{48,112},{56,120},{... | collective-permute-start | bytes 393224 | tf_op jit(solution)/shard_map/ppermute | solution.py:17
  281.3 22.5 %collective-permute-start.1 = (bf16[256,2,128]{0,2,1:T(8,128)(2,1)S(1)}, bf16[256,2,128]{0,2,1:T(8,128)(2,1)S(1)}, u32[]{:S(2)}, u32[]{:S(2)}) collective-permute-start(bf16[256,2,128]{0,2,1:T(8,128)(2,1)S(1)} %bitcast.18), channel_id=1, source_target_pairs={{0,56},{8,64},{16,72},{24,80},{32,88},{40,96},{48,104},{56,112},{6... | collective-permute-start | bytes 393224 | tf_op jit(solution)/shard_map/ppermute | solution.py:17
  282.7 24.0 %collective-permute-start.2 = (bf16[256,2,128]{0,2,1:T(8,128)(2,1)S(1)}, bf16[256,2,128]{0,2,1:T(8,128)(2,1)S(1)}, u32[]{:S(2)}, u32[]{:S(2)}) collective-permute-start(bf16[256,2,128]{0,2,1:T(8,128)(2,1)S(1)} %bitcast.19), channel_id=1, source_target_pairs={{0,48},{8,56},{16,64},{24,72},{32,80},{40,88},{48,96},{56,104},{64... | collective-permute-start | bytes 393224 | tf_op jit(solution)/shard_map/ppermute | solution.py:17
  285.9 23.9 %collective-permute-start.3 = (bf16[256,2,128]{0,2,1:T(8,128)(2,1)S(1)}, bf16[256,2,128]{0,2,1:T(8,128)(2,1)S(1)}, u32[]{:S(2)}, u32[]{:S(2)}) collective-permute-start(bf16[256,2,128]{0,2,1:T(8,128)(2,1)S(1)} %bitcast.20), channel_id=1, source_target_pairs={{0,40},{8,48},{16,56},{24,64},{32,72},{40,80},{48,88},{56,96},{64,... | collective-permute-start | bytes 393224 | tf_op jit(solution)/shard_map/ppermute | solution.py:17
  293.3 18.9 %collective-permute-start.4 = (bf16[256,2,128]{0,2,1:T(8,128)(2,1)S(1)}, bf16[256,2,128]{0,2,1:T(8,128)(2,1)S(1)}, u32[]{:S(2)}, u32[]{:S(2)}) collective-permute-start(bf16[256,2,128]{0,2,1:T(8,128)(2,1)S(1)} %bitcast.21), channel_id=1, source_target_pairs={{0,32},{8,40},{16,48},{24,56},{32,64},{40,72},{48,80},{56,88},{64,... | collective-permute-start | bytes 393224 | tf_op jit(solution)/shard_map/ppermute | solution.py:17
  300.2 16.3 %collective-permute-start.5 = (bf16[256,2,128]{0,2,1:T(8,128)(2,1)S(1)}, bf16[256,2,128]{0,2,1:T(8,128)(2,1)S(1)}, u32[]{:S(2)}, u32[]{:S(2)}) collective-permute-start(bf16[256,2,128]{0,2,1:T(8,128)(2,1)S(1)} %bitcast.22), channel_id=1, source_target_pairs={{0,24},{8,32},{16,40},{24,48},{32,56},{40,64},{48,72},{56,80},{64,... | collective-permute-start | bytes 393224 | tf_op jit(solution)/shard_map/ppermute | solution.py:17
  303.9 15.4 %collective-permute-start.6 = (bf16[256,2,128]{0,2,1:T(8,128)(2,1)S(1)}, bf16[256,2,128]{0,2,1:T(8,128)(2,1)S(1)}, u32[]{:S(2)}, u32[]{:S(2)}) collective-permute-start(bf16[256,2,128]{0,2,1:T(8,128)(2,1)S(1)} %bitcast.23), channel_id=1, source_target_pairs={{0,16},{8,24},{16,32},{24,40},{32,48},{40,56},{48,64},{56,72},{64,... | collective-permute-start | bytes 393224 | tf_op jit(solution)/shard_map/ppermute | solution.py:17
  306.7 14.6 %collective-permute-start.7 = (bf16[256,2,128]{0,2,1:T(8,128)(2,1)S(1)}, bf16[256,2,128]{0,2,1:T(8,128)(2,1)S(1)}, u32[]{:S(2)}, u32[]{:S(2)}) collective-permute-start(bf16[256,2,128]{0,2,1:T(8,128)(2,1)S(1)} %bitcast.24), channel_id=1, source_target_pairs={{0,8},{8,16},{16,24},{24,32},{32,40},{40,48},{48,56},{56,64},{64,7... | collective-permute-start | bytes 393224 | tf_op jit(solution)/shard_map/ppermute | solution.py:17
  309.8 15.9 %collective-permute-start.16 = (bf16[256,2,128]{2,0,1:T(8,128)(2,1)S(1)}, bf16[256,2,128]{2,0,1:T(8,128)(2,1)S(1)}, u32[]{:S(2)}, u32[]{:S(2)}) collective-permute-start(bf16[256,2,128]{2,0,1:T(8,128)(2,1)S(1)} %maximum_convert_fusion), channel_id=1, source_target_pairs={{0,64},{8,72},{16,80},{24,88},{32,96},{40,104},{48,112},{56,120},{... | collective-permute-start | bytes 393224 | tf_op jit(solution)/shard_map/ppermute | solution.py:17
  312.1 16.3 %collective-permute-start.17 = (bf16[256,2,128]{2,0,1:T(8,128)(2,1)S(1)}, bf16[256,2,128]{2,0,1:T(8,128)(2,1)S(1)}, u32[]{:S(2)}, u32[]{:S(2)}) collective-permute-start(bf16[256,2,128]{2,0,1:T(8,128)(2,1)S(1)} %maximum_convert_fusion), channel_id=1, source_target_pairs={{0,56},{8,64},{16,72},{24,80},{32,88},{40,96},{48,104},{56,112},{6... | collective-permute-start | bytes 393224 | tf_op jit(solution)/shard_map/ppermute | solution.py:17
  316.5 14.8 %collective-permute-start.18 = (bf16[256,2,128]{2,0,1:T(8,128)(2,1)S(1)}, bf16[256,2,128]{2,0,1:T(8,128)(2,1)S(1)}, u32[]{:S(2)}, u32[]{:S(2)}) collective-permute-start(bf16[256,2,128]{2,0,1:T(8,128)(2,1)S(1)} %maximum_convert_fusion), channel_id=1, source_target_pairs={{0,48},{8,56},{16,64},{24,72},{32,80},{40,88},{48,96},{56,104},{64... | collective-permute-start | bytes 393224 | tf_op jit(solution)/shard_map/ppermute | solution.py:17
  319.3 15.4 %collective-permute-start.19 = (bf16[256,2,128]{2,0,1:T(8,128)(2,1)S(1)}, bf16[256,2,128]{2,0,1:T(8,128)(2,1)S(1)}, u32[]{:S(2)}, u32[]{:S(2)}) collective-permute-start(bf16[256,2,128]{2,0,1:T(8,128)(2,1)S(1)} %maximum_convert_fusion), channel_id=1, source_target_pairs={{0,40},{8,48},{16,56},{24,64},{32,72},{40,80},{48,88},{56,96},{64,... | collective-permute-start | bytes 393224 | tf_op jit(solution)/shard_map/ppermute | solution.py:17
  321.3 13.5 %collective-permute-start.20 = (bf16[256,2,128]{2,0,1:T(8,128)(2,1)S(1)}, bf16[256,2,128]{2,0,1:T(8,128)(2,1)S(1)}, u32[]{:S(2)}, u32[]{:S(2)}) collective-permute-start(bf16[256,2,128]{2,0,1:T(8,128)(2,1)S(1)} %maximum_convert_fusion), channel_id=1, source_target_pairs={{0,32},{8,40},{16,48},{24,56},{32,64},{40,72},{48,80},{56,88},{64,... | collective-permute-start | bytes 393224 | tf_op jit(solution)/shard_map/ppermute | solution.py:17
  325.6 12.0 %copy-start.5 = (bf16[2304,2,128]{0,2,1:T(8,128)(2,1)}, bf16[2304,2,128]{0,2,1:T(8,128)(2,1)S(1)}, u32[]{:S(2)}) copy-start(bf16[2304,2,128]{0,2,1:T(8,128)(2,1)S(1)} %constant_dynamic-update-slice_fusion.7) | copy-start | bytes 3538948
  325.7 9.2 %collective-permute-start.21 = (bf16[256,2,128]{2,0,1:T(8,128)(2,1)S(1)}, bf16[256,2,128]{2,0,1:T(8,128)(2,1)S(1)}, u32[]{:S(2)}, u32[]{:S(2)}) collective-permute-start(bf16[256,2,128]{2,0,1:T(8,128)(2,1)S(1)} %maximum_convert_fusion), channel_id=1, source_target_pairs={{0,24},{8,32},{16,40},{24,48},{32,56},{40,64},{48,72},{56,80},{64,... | collective-permute-start | bytes 393224 | tf_op jit(solution)/shard_map/ppermute | solution.py:17
  328.5 7.7 %collective-permute-start.22 = (bf16[256,2,128]{2,0,1:T(8,128)(2,1)S(1)}, bf16[256,2,128]{2,0,1:T(8,128)(2,1)S(1)}, u32[]{:S(2)}, u32[]{:S(2)}) collective-permute-start(bf16[256,2,128]{2,0,1:T(8,128)(2,1)S(1)} %maximum_convert_fusion), channel_id=1, source_target_pairs={{0,16},{8,24},{16,32},{24,40},{32,48},{40,56},{48,64},{56,72},{64,... | collective-permute-start | bytes 393224 | tf_op jit(solution)/shard_map/ppermute | solution.py:17
  331.3 6.3 %collective-permute-start.23 = (bf16[256,2,128]{2,0,1:T(8,128)(2,1)S(1)}, bf16[256,2,128]{2,0,1:T(8,128)(2,1)S(1)}, u32[]{:S(2)}, u32[]{:S(2)}) collective-permute-start(bf16[256,2,128]{2,0,1:T(8,128)(2,1)S(1)} %maximum_convert_fusion), channel_id=1, source_target_pairs={{0,8},{8,16},{16,24},{24,32},{32,40},{40,48},{48,56},{56,64},{64,7... | collective-permute-start | bytes 393224 | tf_op jit(solution)/shard_map/ppermute | solution.py:17
  337.7 1.0 copy-start.7
  338.7 6.1 %copy-start.6 = (bf16[2304,2,128]{0,2,1:T(8,128)(2,1)S(1)}, bf16[2304,2,128]{0,2,1:T(8,128)(2,1)}, u32[]{:S(2)}) copy-start(bf16[2304,2,128]{0,2,1:T(8,128)(2,1)} %copy-done.5) | copy-start | bytes 3538948
  348.1 41.1 %copy-start.4 = (bf16[256,256]{1,0:T(8,128)(2,1)S(1)}, bf16[256,256]{1,0:T(8,128)(2,1)}, u32[]{:S(2)}) copy-start(bf16[256,256]{1,0:T(8,128)(2,1)} %param.10) | copy-start | bytes 393220
  350.9 82.2 %all-gather.5.cloned.1.call-start = ((), (), s32[]{:S(2)}) async-start(), calls=%async_computation.5 | async-start | bytes 1179648 | tf_op jit(solution)/shard_map/all_gather | solution.py:118
  390.7 93.2 %reduce-scatter.5.cloned.1.call-start = ((), (), s32[]{:S(2)}) async-start(), calls=%async_computation.6 | async-start | bytes 1179648 | tf_op jit(solution)/shard_map/reduce_scatter | solution.py:126
  433.1 3.2 copy-start.1
  438.7 4.7 copy-start.9
  443.3 40.6 %copy-start.2 = (bf16[256,256]{1,0:T(8,128)(2,1)S(1)}, bf16[256,256]{1,0:T(8,128)(2,1)}, u32[]{:S(2)}) copy-start(bf16[256,256]{1,0:T(8,128)(2,1)} %add_convert_fusion.1) | copy-start | bytes 393220
  444.9 40.6 %copy-start.3 = (bf16[2,16,16,256]{3,2,1,0:T(8,128)(2,1)}, bf16[2,16,16,256]{3,2,1,0:T(8,128)(2,1)S(1)}, u32[]{:S(2)}) copy-start(bf16[2,16,16,256]{3,2,1,0:T(8,128)(2,1)S(1)} %scatter_fusion) | copy-start | bytes 786436
Sparse Core Ops, SparseCore 0:
  51.2 38.1 all-gather.2
  351.0 38.0 reduce-scatter.2
  391.7 41.3 all-gather.4
  443.5 40.3 reduce-scatter.4
